TPU v7x, 256 devices: a whole 4x4x8 slice. The times are simulated.
256 devices in a mesh: tile: 32 (over x, z), atom: 8 (over y, core).
Axes of the slice: x: 4, y: 4, z: 8, core: 2. Of those that a mesh axis runs over, the one named last changes fastest.
Arguments:
- images: float32 [1024, 1024], P(('tile', 'atom')), may hold values from -6 to 6
- active: int32 [1024, 2], P(('tile', 'atom')), may hold values from 0 to 7, all different within a row; in each aligned block of 4 rows (0 to 3, 4 to 7, ...) at most 2 rows name the same one
- dictionary: float32 [8, 32, 1024], P('atom', 'tile'), may hold values from -6 to 6
Outputs:
- reconstruction: float32 [1024, 1024], P(('tile', 'atom'))
- new_dictionary: float32 [8, 32, 1024], P('atom', 'tile')
Inputs may be any that keep to these rules, and one draw needn't show every extreme that they name: `active`: each tile names 2 different atom blocks. Among the 4 tiles of one device no block is named by more than 2 tiles, and on some devices one block is named by exactly 2. Every block is named by some tile.
All inputs are finite; a program needn't handle non-finite values.
Results may differ from a plain program's by a relative error of at most 0.0001.
Values sent between devices are 32-bit elements; how exact they have to be, the bound alone decides.
No kernel may reach another device: no remote copies, remote signals or barrier semaphores. Data moves between devices by JAX's collectives and lax.ppermute only.
A program may use at most 128 MiB of HBM per device.

v0:
```python
import math
import jax
import jax.numpy as jnp
from jax import lax
from jax.sharding import PartitionSpec as P

SIDE = 32
BLK = 32
NBLK = 8
ACT = 2
MOST = 2
ITERS = 2
shrink_scale = 0.5
step_ratio = 0.5
epsilon = 1e-06
highest = lax.Precision.HIGHEST


def momentum_weights(count):
    weights = []
    current = 1.0
    for sweep in range(count):
        following = (1.0 + math.sqrt(1.0 + 4.0 * current * current)) / 2.0
        weights.append((current - 1.0) / following)
        current = following
    return weights


def unit_rows(values):
    return values / jnp.sqrt(jnp.mean(values * values, axis=-1, keepdims=True) + epsilon)


def fourier_table(length):
    position = jnp.arange(length, dtype=jnp.int32)
    phase = position[:, None] * position[None, :] % length
    angle = phase.astype(jnp.float32) * (2.0 * math.pi / length)
    cosine = jnp.cos(angle)
    sine = jnp.sin(angle)
    forward_right = jnp.stack([cosine, -sine], axis=1)
    forward_left = jnp.stack(
        [jnp.stack([cosine, sine], axis=1), jnp.stack([-sine, cosine], axis=1)], axis=0
    )
    inverse_right = jnp.stack(
        [jnp.stack([cosine, sine], axis=1), jnp.stack([-sine, cosine], axis=1)], axis=0
    )
    inverse_left = jnp.stack([cosine, -sine], axis=0)
    return (forward_right, forward_left, inverse_right, inverse_left)


def forward(values, table):
    forward_right, forward_left = (table[0], table[1])
    length = forward_right.shape[0]
    field = values.reshape(values.shape[:-1] + (length, length))
    across = jnp.einsum(
        "...uw,wdq->...udq",
        field,
        forward_right,
        precision=highest,
        preferred_element_type=jnp.float32,
    )
    result = jnp.einsum(
        "cpdu,...udq->...cpq",
        forward_left,
        across,
        precision=highest,
        preferred_element_type=jnp.float32,
    )
    return result.reshape(values.shape[:-1] + (2 * length * length,))


def inverse(spectra, table):
    inverse_right, inverse_left = (table[2], table[3])
    length = inverse_left.shape[1]
    shaped = spectra.reshape(spectra.shape[:-1] + (2, length, length))
    across = jnp.einsum(
        "...cpq,cqew->...pew",
        shaped,
        inverse_right,
        precision=highest,
        preferred_element_type=jnp.float32,
    )
    result = jnp.einsum(
        "lmq,...qlg->...mg",
        inverse_left,
        across,
        precision=highest,
        preferred_element_type=jnp.float32,
    )
    return result.reshape(spectra.shape[:-1] + (length * length,)) / (length * length)


def split_parts(packed):
    middle = packed.shape[-1] // 2
    return (packed[..., :middle], packed[..., middle:])


def times_conj(first, second):
    first_real, first_imag = split_parts(first)
    second_real, second_imag = split_parts(second)
    real_part = first_real * second_real + first_imag * second_imag
    imag_part = first_real * second_imag - first_imag * second_real
    return jnp.concatenate([real_part, imag_part], axis=-1)


def product_sum(atom_spec, code_spec):
    atom_real, atom_imag = split_parts(atom_spec)
    code_real, code_imag = split_parts(code_spec)
    real_sum = jnp.sum(atom_real * code_real - atom_imag * code_imag, axis=(1, 2))
    imag_sum = jnp.sum(atom_real * code_imag + atom_imag * code_real, axis=(1, 2))
    return jnp.concatenate([real_sum, imag_sum], axis=-1)


def on_device(images, active, dictionary):
    tiles_here = images.shape[0]
    pixels = images.shape[1]
    rows_owned = dictionary.shape[1]
    table = fourier_table(SIDE)
    image_spec = forward(images, table)
    atoms = unit_rows(dictionary)
    slot_count = tiles_here * ACT
    flat_ids = active.reshape(slot_count)
    block_range = jnp.arange(NBLK, dtype=jnp.int32)
    slot_index = jnp.arange(slot_count, dtype=jnp.int32)
    earlier = slot_index[None, :] < slot_index[:, None]
    same_block = flat_ids[:, None] == flat_ids[None, :]
    rank = jnp.sum((earlier & same_block).astype(jnp.int32), axis=1)
    slot_range = jnp.arange(MOST, dtype=jnp.int32)
    placing = (block_range[:, None, None] == flat_ids[None, None, :]) & (
        slot_range[None, :, None] == rank[None, None, :]
    )
    placing = placing.astype(jnp.float32).reshape(NBLK * MOST, slot_count)
    codes = jnp.zeros((tiles_here, ACT, BLK, pixels), jnp.float32)
    code_spec = jnp.zeros((tiles_here, ACT, BLK, 2 * pixels), jnp.float32)
    weights = momentum_weights(ITERS)
    own_spec = forward(atoms, table)
    every = lax.all_gather(own_spec, ("tile", "atom"), axis=0, tiled=True)
    tile_groups = lax.axis_size("tile")
    every = every.reshape(tile_groups, NBLK, rows_owned, 2 * pixels)
    chosen = jnp.take(every, flat_ids, axis=1)
    chosen = jnp.transpose(chosen, (1, 0, 2, 3)).reshape(tiles_here, ACT, BLK, 2 * pixels)
    chosen_real, chosen_imag = split_parts(chosen)
    power = chosen_real * chosen_real + chosen_imag * chosen_imag
    bound = jnp.max(jnp.sum(power, axis=(1, 2)), axis=1) + epsilon
    rate = (1.0 / bound)[:, None, None, None]
    limit = rate * (shrink_scale * SIDE)
    prior = codes
    prior_spec = code_spec
    guess = codes
    guess_spec = code_spec
    for sweep in range(ITERS):
        residual_spec = product_sum(chosen, guess_spec) - image_spec
        gradient = inverse(times_conj(chosen, residual_spec[:, None, None, :]), table)
        moved = guess - rate * gradient
        fresh = moved - jnp.clip(moved, -limit, limit)
        fresh_spec = forward(fresh, table)
        guess = fresh + weights[sweep] * (fresh - prior)
        guess_spec = fresh_spec + weights[sweep] * (fresh_spec - prior_spec)
        prior, prior_spec = (fresh, fresh_spec)
    recon_spec = product_sum(chosen, prior_spec)
    residual_spec = recon_spec - image_spec
    slot_terms = times_conj(prior_spec, residual_spec[:, None, None, :]).reshape(
        slot_count, BLK * 2 * pixels
    )
    outgoing = jnp.dot(placing, slot_terms, precision=highest, preferred_element_type=jnp.float32)
    outgoing = outgoing.reshape(NBLK, MOST, BLK, 2 * pixels)
    arrived = lax.all_to_all(outgoing, "atom", split_axis=0, concat_axis=1, tiled=True)
    owner_sum = jnp.sum(arrived, axis=1)
    total = lax.psum(owner_sum, "tile")
    offset = lax.axis_index("tile") * rows_owned
    mine = lax.dynamic_slice_in_dim(total, offset, rows_owned, 1)
    atom_grad = inverse(mine, table)
    scale = jnp.sqrt(jnp.mean(atom_grad * atom_grad, axis=-1, keepdims=True) + epsilon)
    atoms = unit_rows(atoms - step_ratio * atom_grad / scale)
    recon = inverse(recon_spec, table)
    return (recon, atoms)


def solution(mesh):
    in_specs = (P(("tile", "atom"), None), P(("tile", "atom"), None), P("atom", "tile", None))
    out_specs = (P(("tile", "atom"), None), P("atom", "tile", None))
    return jax.shard_map(
        on_device, mesh=mesh, in_specs=in_specs, out_specs=out_specs, check_vma=False
    )
```

profile of v0, /device:TPU:8, one launch (start us, length us, event | category | flops | bytes accessed | tf_op | source)
XLA Modules:
  0.0 500.6 jit_solution(15187165786976593706)
XLA Ops:
  7.2 0.1 fusion.71
  7.3 0.1 fusion.70
  7.4 1.3 multiply_reduce_fusion.2
  9.4 0.5 broadcast.415
  9.9 1.3 fusion.91
  11.3 0.2 convolution_bitcast_fusion.6
  11.6 0.3 convolution_bitcast_fusion.5
  11.9 0.7 reshape.499
  12.6 0.8 copy.66
  13.4 0.1 reshape.501
  13.5 0.1 reshape.497
  13.6 0.8 reshape.527
  14.4 0.5 convolution_bitcast_fusion.2
  14.9 0.3 convolution_bitcast_fusion.1
  15.2 0.1 copy.72
  15.3 0.1 reshape.504
  15.4 0.1 sine_negate_fusion
  15.5 0.2 convert_reduce_fusion
  15.7 104.0 %all-gather.2.cloned.1.call-done = f32[256,1,2048]{2,1,0:T(1,128)} async-done(((f32[1,1,2048]{2,1,0:T(1,128)}), f32[256,1,2048]{2,1,0:T(1,128)}) %all-gather.2.cloned.1.call-update) | async-done | bytes 2097168 | tf_op jit(solution)/shard_map/all_gather | solution.py:136
  119.8 2.5 copy.160
  122.2 1.2 copy.70
  123.5 2.0 gather_fusion
  125.5 1.9 bitcast_select_fusion
  127.4 0.4 add_reduce_fusion.2
  127.9 0.3 multiply_add_fusion.4
  128.2 1.5 pad_maximum_fusion
  129.7 6.5 %reshape.531 = f32[4,2,32,2,32,32,1]{5,4,3,2,1,0,6:T(8,128)} reshape(f32[4,2,32,2048]{3,2,1,0:T(8,128)} %pad_maximum_fusion) | data formatting | bytes 4194304 | tf_op jit(solution)/shard_map/reshape | solution.py:74
  136.2 23.9 %fusion.6 = f32[4,2,32,32,2,32,1]{3,5,4,6,2,1,0:T(8,128)} fusion(f32[4,2,32,2,32,32,1]{5,4,3,2,1,0,6:T(8,128)} %reshape.531, f32[1,32,2,32]{3,1,2,0:T(8,128)S(1)} %get-tuple-element.28, f32[1,32,2,32]{3,1,2,0:T(8,128)S(1)} %get-tuple-element.27), kind=kOutput, calls=%fused_computation.7 | convolution fusion | flops 402657280 | bytes 4210688 | tf_op jit(solution)/shard_map/...cpq,cqew->...pew/dot_general | solution.py:75
  160.1 0.1 reduce_max.9
  160.2 10.9 %fusion.4 = f32[4,2,32,32,32,1]{4,3,5,2,1,0:T(8,128)S(1)} fusion(f32[4,2,32,32,2,32,1]{3,5,4,6,2,1,0:T(8,128)} %fusion.6, f32[1,32,32]{2,1,0:T(8,128)S(1)} %get-tuple-element.35, f32[1,32,32]{2,1,0:T(8,128)S(1)} %get-tuple-element.36), kind=kOutput, calls=%fused_computation.5 | convolution fusion | flops 201328640 | bytes 3153920 | tf_op jit(solution)/shard_map/lmq,...qlg->...mg/dot_general | solution.py:82
  171.2 7.1 %fusion.15 = f32[4,2,32,32,2,32]{3,5,4,2,1,0:T(8,128)S(1)} fusion(f32[4,2,32,32,32,1]{4,3,5,2,1,0:T(8,128)S(1)} %fusion.4, f32[4]{0:T(128)S(1)} %get-tuple-element.30, f32[4]{0:T(128)S(1)} %get-tuple-element.29, f32[4]{0:T(128)S(1)} %get-tuple-element.11, f32[32,1,32]{2,0,1:T(8,128)S(1)} %get-tuple-element.33, f32[32,1,32]{2,0,1:T(8,128)S(1)} %get-tuple-element.34), kind=kOutput, calls=%fused_computation.17 | convolution fusion | flops 202639360 | bytes 3153968 | tf_op jit(solution)/shard_map/...uw,wdq->...udq/dot_general | solution.py:54
  178.4 8.9 %fusion.23 = f32[4,2,32,2,32,32]{4,5,3,2,1,0:T(8,128)} fusion(f32[4,2,32,32,2,32]{3,5,4,2,1,0:T(8,128)S(1)} %fusion.15, f32[1,32,2,32]{3,1,2,0:T(8,128)S(1)} %get-tuple-element.28, f32[1,32,2,32]{3,1,2,0:T(8,128)S(1)} %get-tuple-element.27), kind=kOutput, calls=%fused_computation.28 | convolution fusion | flops 402657280 | bytes 4210688 | tf_op jit(solution)/shard_map/cpdu,...udq->...cpq/dot_general | solution.py:61
  187.3 8.9 %copy.78 = f32[4,2,32,2,32,32]{5,4,3,2,1,0:T(8,128)} copy(f32[4,2,32,2,32,32]{4,5,3,2,1,0:T(8,128)} %fusion.23) | data formatting | bytes 4194304 | tf_op jit(solution)/shard_map/cpdu,...udq->...cpq/transpose | solution.py:61
  196.2 7.6 %reshape.506 = f32[4,2,32,2048]{3,2,1,0:T(8,128)} reshape(f32[4,2,32,2,32,32]{5,4,3,2,1,0:T(8,128)} %copy.78) | data formatting | bytes 4194304 | tf_op jit(solution)/shard_map/reshape | solution.py:68
  203.9 1.8 multiply_add_fusion.1
  205.6 0.6 subtract_reduce_fusion.1
  206.2 0.3 multiply_add_fusion.3
  206.5 1.5 pad_maximum_fusion.1
  208.1 6.3 %reshape.541 = f32[4,2,32,2,32,32,1]{5,4,3,2,1,0,6:T(8,128)} reshape(f32[4,2,32,2048]{3,2,1,0:T(8,128)} %pad_maximum_fusion.1) | data formatting | bytes 4194304 | tf_op jit(solution)/shard_map/reshape | solution.py:74
  214.3 22.6 %fusion.2 = f32[4,2,32,32,2,32,1]{3,5,4,6,2,1,0:T(8,128)S(1)} fusion(f32[4,2,32,2,32,32,1]{5,4,3,2,1,0,6:T(8,128)} %reshape.541, f32[1,32,2,32]{3,1,2,0:T(8,128)S(1)} %get-tuple-element.28, f32[1,32,2,32]{3,1,2,0:T(8,128)S(1)} %get-tuple-element.27), kind=kOutput, calls=%fused_computation.3 | convolution fusion | flops 402657280 | bytes 4210688 | tf_op jit(solution)/shard_map/...cpq,cqew->...pew/dot_general | solution.py:75
  237.0 6.7 %fusion = f32[4,2,32,32,32,1]{4,3,5,2,1,0:T(8,128)S(1)} fusion(f32[4,2,32,32,2,32,1]{3,5,4,6,2,1,0:T(8,128)S(1)} %fusion.2, f32[1,32,32]{2,1,0:T(8,128)S(1)} %get-tuple-element.35, f32[1,32,32]{2,1,0:T(8,128)S(1)} %get-tuple-element.36), kind=kOutput, calls=%fused_computation.1 | convolution fusion | flops 201328640 | bytes 3153920 | tf_op jit(solution)/shard_map/lmq,...qlg->...mg/dot_general | solution.py:82
  243.6 8.9 %fusion.13 = f32[4,2,32,32,2,32]{3,5,4,2,1,0:T(8,128)S(1)} fusion(f32[4,2,32,32,32,1]{4,3,5,2,1,0:T(8,128)S(1)} %fusion, f32[4,2,32,32,32,1]{4,3,5,2,1,0:T(8,128)S(1)} %copy-done.1, f32[4]{0:T(128)S(1)} %get-tuple-element.30, f32[4]{0:T(128)S(1)} %get-tuple-element.29, f32[4]{0:T(128)S(1)} %get-tuple-element.11, f32[32,1,32]{2,0,1:T(8,128)S(1)} %get-tuple-element.33, ...), kind=kOutput, calls=%fused_computation.15 | convolution fusion | flops 204474368 | bytes 4202544 | tf_op jit(solution)/shard_map/...uw,wdq->...udq/dot_general | solution.py:54
  252.5 8.9 %fusion.26 = f32[4,2,32,2,32,32]{4,5,3,2,1,0:T(8,128)} fusion(f32[4,2,32,32,2,32]{3,5,4,2,1,0:T(8,128)S(1)} %fusion.13, f32[1,32,2,32]{3,1,2,0:T(8,128)S(1)} %get-tuple-element.28, f32[1,32,2,32]{3,1,2,0:T(8,128)S(1)} %get-tuple-element.27), kind=kOutput, calls=%fused_computation.29 | convolution fusion | flops 402657280 | bytes 4210688 | tf_op jit(solution)/shard_map/cpdu,...udq->...cpq/dot_general | solution.py:61
  261.5 8.9 %copy.83 = f32[4,2,32,2,32,32]{5,4,3,2,1,0:T(8,128)} copy(f32[4,2,32,2,32,32]{4,5,3,2,1,0:T(8,128)} %fusion.26) | data formatting | bytes 4194304 | tf_op jit(solution)/shard_map/cpdu,...udq->...cpq/transpose | solution.py:61
  270.4 7.7 %reshape.508 = f32[4,2,32,2048]{3,2,1,0:T(8,128)} reshape(f32[4,2,32,2,32,32]{5,4,3,2,1,0:T(8,128)} %copy.83) | data formatting | bytes 4194304 | tf_op jit(solution)/shard_map/reshape | solution.py:68
  278.1 2.3 subtract_reduce_fusion
  280.4 0.4 multiply_add_fusion.2
  280.9 0.2 pad_maximum_fusion.2
  281.1 2.7 fusion.72
  283.8 4.4 copy.87
  288.2 4.9 all-to-all-start
  293.2 0.1 reshape.548
  293.3 48.2 %all-to-all-done = f32[8,2,32,2048]{3,2,1,0:T(8,128)} async-done(((f32[8,2,32,2048]{3,2,1,0:T(8,128)}), f32[8,2,32,2048]{3,2,1,0:T(8,128)}, u32[]{:S(2)}, u32[]{:S(2)}) %all-to-all-start) | async-done | bytes 4194336 | tf_op jit(solution)/shard_map/all_to_all | solution.py:166
  341.5 3.1 reduce_sum.119
  344.6 0.5 convolution_bitcast_fusion
  345.1 0.3 fusion.39
  345.5 0.7 div.88
  346.2 142.3 %all-reduce.2.cloned.1.call-done = f32[1,32,2048]{2,1,0:T(8,128)} async-done(((f32[1,32,2048]{2,1,0:T(8,128)}), f32[1,32,2048]{2,1,0:T(8,128)}) %all-reduce.2.cloned.1.call-update) | async-done | bytes 262160 | tf_op jit(solution)/shard_map/psum | solution.py:168
  488.5 0.9 dynamic-slice_reduce_fusion
  489.5 0.3 convolution_bitcast_fusion.4
  489.8 0.8 multiply_reduce_fusion
  491.3 0.1 div.96
  491.4 0.6 multiply_reduce_fusion.1
  492.7 0.6 broadcast_divide_fusion
  (31 shorter events, 0.6 us)
Async XLA Ops:
  7.2 112.6 %all-gather.2.cloned.1.call-start = ((), (), s32[]{:S(2)}) async-start(), calls=%async_computation.1 | async-start | bytes 2105344 | tf_op jit(solution)/shard_map/all_gather | solution.py:136
  171.2 7.2 %copy-start = (f32[4,2,32,32,32,1]{4,3,5,2,1,0:T(8,128)}, f32[4,2,32,32,32,1]{4,3,5,2,1,0:T(8,128)S(1)}, u32[]{:S(2)}) copy-start(f32[4,2,32,32,32,1]{4,3,5,2,1,0:T(8,128)S(1)} %fusion.4) | copy-start | bytes 3145732
  237.0 6.7 %copy-start.1 = (f32[4,2,32,32,32,1]{4,3,5,2,1,0:T(8,128)S(1)}, f32[4,2,32,32,32,1]{4,3,5,2,1,0:T(8,128)}, u32[]{:S(2)}) copy-start(f32[4,2,32,32,32,1]{4,3,5,2,1,0:T(8,128)} %copy-done) | copy-start | bytes 3145732
  278.1 2.3 copy-start.2
  288.2 53.3 %all-to-all-start = ((f32[8,2,32,2048]{3,2,1,0:T(8,128)}), f32[8,2,32,2048]{3,2,1,0:T(8,128)}, u32[]{:S(2)}, u32[]{:S(2)}) async-start(f32[8,2,32,2048]{3,2,1,0:T(8,128)} %copy.87), calls=%async_computation | async-start | bytes 8388608 | tf_op jit(solution)/shard_map/all_to_all | solution.py:166
  293.2 195.3 %all-reduce.2.cloned.1.call-start = ((), (), s32[]{:S(2)}) async-start(), calls=%async_computation.2 | async-start | bytes 524288 | tf_op jit(solution)/shard_map/psum | solution.py:168
Sparse Core Ops, SparseCore 0:
  12.8 106.9 all-gather.1
  344.8 143.7 all-reduce.1
where the time goes:
time: 506 us; the launch traced here: 501 us
  waiting for transfers between devices  295 us (58%)
  matrix products  104 us (21%)
  local copies, waits for them, and re-layouts  61.4 us (12%)
  other arithmetic  18.9 us (4%)
  between operations  16.9 us (3%)
    psum x1, waiting for transfers between devices, on_device(): total = lax.psum(owner_sum, 'tile')  142 us
    all_gather x1, waiting for transfers between devices, on_device(): every = lax.all_gather(own_spec, ('tile', 'atom'), axis=0, tiled=True)  104 us
    all_to_all x1, waiting for transfers between devices, on_device(): lax.all_to_all(outgoing, 'atom', split_axis=0, concat_axis=1, tiled=True)  48.2 us
    dot_general x4, matrix products, inverse(): jnp.einsum('...cpq,cqew->...pew', shaped, inverse_right, precision=highes...  47.3 us
    dot_general x4, matrix products, inverse(): jnp.einsum('lmq,...qlg->...mg', inverse_left, across, precision=highest,...  18.6 us
    dot_general x4, matrix products, forward(): jnp.einsum('cpdu,...udq->...cpq', forward_left, across, precision=highest...  18.4 us
    transpose x4, local copies, waits for them, and re-layouts, forward(): jnp.einsum('cpdu,...udq->...cpq', forward_left, across, precision=highest...  18 us
    dot_general x4, matrix products, forward(): jnp.einsum('...uw,wdq->...udq', field, forward_right, precision=highest,...  16.8 us
  transfers between devices with their start and end apart: 3, of which 3 were waited for; matrix products, arithmetic and copies ran while one was open for 1% of the time, Pallas kernels for 0%

commit v1 on v0

--- a/solution.py
+++ b/solution.py
@@ -133,7 +133,12 @@
     code_spec = jnp.zeros((tiles_here, ACT, BLK, 2 * pixels), jnp.float32)
     weights = momentum_weights(ITERS)
     own_spec = forward(atoms, table)
-    every = lax.all_gather(own_spec, ("tile", "atom"), axis=0, tiled=True)
+    every = jnp.concatenate(
+        lax.all_to_all(
+            jnp.stack([own_spec] * lax.axis_size(("tile", "atom"))), ("tile", "atom"), 0, 0
+        ),
+        axis=0,
+    )
     tile_groups = lax.axis_size("tile")
     every = every.reshape(tile_groups, NBLK, rows_owned, 2 * pixels)
     chosen = jnp.take(every, flat_ids, axis=1)

time: 506 us -> 468 us (0.925)
  waiting for transfers between devices: 295 us -> 240 us
  starting transfers between devices: 4.99 us -> 19.5 us
    all_gather x1 -> x0, waiting for transfers between devices: 104 us -> none  [on_device(): every = lax.all_gather(own_spec, ('tile', 'atom'), axis=0, tiled=True)]
    all_to_all x0 -> x1, waiting for transfers between devices: none -> 51.9 us  [on_device(): lax.all_to_all(jnp.stack([own_spec] * lax.axis_size(('tile', 'atom'))), (...]
    all_to_all x0 -> x1, starting transfers between devices: none -> 14.6 us  [on_device(): lax.all_to_all(jnp.stack([own_spec] * lax.axis_size(('tile', 'atom'))), (...]
    reshape x4 -> x3, local copies, waits for them, and re-layouts: 16.2 us -> 15.3 us  [forward(): return result.reshape(values.shape[:-1] + (2 * length * length,))]
where the time goes in v1:
time: 468 us; the launch traced here: 459 us
  waiting for transfers between devices  240 us (51%)
  matrix products  104 us (22%)
  local copies, waits for them, and re-layouts  59.8 us (13%)
  starting transfers between devices  19.5 us (4%)
  other arithmetic  18.9 us (4%)
  between operations  16.9 us (4%)
    psum x1, waiting for transfers between devices, on_device(): total = lax.psum(owner_sum, 'tile')  139 us
    all_to_all x1, waiting for transfers between devices, on_device(): lax.all_to_all(jnp.stack([own_spec] * lax.axis_size(('tile', 'atom'))), (...  51.9 us
    all_to_all x1, waiting for transfers between devices, on_device(): lax.all_to_all(outgoing, 'atom', split_axis=0, concat_axis=1, tiled=True)  48.2 us
    dot_general x4, matrix products, inverse(): jnp.einsum('...cpq,cqew->...pew', shaped, inverse_right, precision=highes...  47.5 us
    dot_general x4, matrix products, forward(): jnp.einsum('cpdu,...udq->...cpq', forward_left, across, precision=highest...  18.8 us
    dot_general x4, matrix products, inverse(): jnp.einsum('lmq,...qlg->...mg', inverse_left, across, precision=highest,...  18.4 us
    transpose x4, local copies, waits for them, and re-layouts, forward(): jnp.einsum('cpdu,...udq->...cpq', forward_left, across, precision=highest...  18 us
    dot_general x4, matrix products, forward(): jnp.einsum('...uw,wdq->...udq', field, forward_right, precision=highest,...  16.8 us
  transfers between devices with their start and end apart: 3, of which 3 were waited for; matrix products, arithmetic and copies ran while one was open for 1% of the time, Pallas kernels for 0%

profile of v1, /device:TPU:8, one launch (start us, length us, event | category | flops | bytes accessed | tf_op | source)
XLA Modules:
  0.0 458.9 jit_solution(4038994808032598931)
XLA Ops:
  7.2 0.1 fusion.71
  7.3 0.1 fusion.70
  7.4 1.3 multiply_reduce_fusion.2
  9.4 0.5 broadcast.417
  9.9 1.3 fusion.91
  11.3 0.2 convolution_bitcast_fusion.6
  11.6 0.3 convolution_bitcast_fusion.5
  12.0 2.4 stack.22
  14.4 14.6 %all-to-all-start = ((f32[256,1,1,2048]{3,2,1,0:T(1,128)}), f32[256,1,1,2048]{3,2,1,0:T(1,128)S(1)}, u32[]{:S(2)}, u32[]{:S(2)}) async-start(f32[256,1,1,2048]{3,2,1,0:T(1,128)} %stack.22), calls=%async_computation | async-start | bytes 4194304 | tf_op jit(solution)/shard_map/all_to_all | solution.py:137
  29.0 0.1 copy.66
  29.1 0.1 reshape.497
  29.3 0.1 reshape.523
  29.4 0.5 convolution_bitcast_fusion.2
  29.9 0.3 convolution_bitcast_fusion.1
  30.2 0.1 copy.72
  30.3 0.1 reshape.500
  30.4 0.1 sine_negate_fusion
  30.5 0.2 convert_reduce_fusion
  30.8 51.9 %all-to-all-done = f32[256,1,1,2048]{3,2,1,0:T(1,128)S(1)} async-done(((f32[256,1,1,2048]{3,2,1,0:T(1,128)}), f32[256,1,1,2048]{3,2,1,0:T(1,128)S(1)}, u32[]{:S(2)}, u32[]{:S(2)}) %all-to-all-start) | async-done | bytes 2097184 | tf_op jit(solution)/shard_map/all_to_all | solution.py:137
  82.7 0.9 copy.160
  83.6 1.2 copy.70
  84.8 2.0 gather_fusion
  86.8 1.9 bitcast_select_fusion
  88.7 0.4 add_reduce_fusion.2
  89.2 0.3 multiply_add_fusion.4
  89.5 1.5 pad_maximum_fusion
  91.0 6.3 %reshape.527 = f32[4,2,32,2,32,32,1]{5,4,3,2,1,0,6:T(8,128)} reshape(f32[4,2,32,2048]{3,2,1,0:T(8,128)} %pad_maximum_fusion) | data formatting | bytes 4194304 | tf_op jit(solution)/shard_map/reshape | solution.py:74
  97.3 23.9 %fusion.6 = f32[4,2,32,32,2,32,1]{3,5,4,6,2,1,0:T(8,128)} fusion(f32[4,2,32,2,32,32,1]{5,4,3,2,1,0,6:T(8,128)} %reshape.527, f32[1,32,2,32]{3,1,2,0:T(8,128)S(1)} %get-tuple-element.28, f32[1,32,2,32]{3,1,2,0:T(8,128)S(1)} %get-tuple-element.27), kind=kOutput, calls=%fused_computation.7 | convolution fusion | flops 402657280 | bytes 4210688 | tf_op jit(solution)/shard_map/...cpq,cqew->...pew/dot_general | solution.py:75
  121.2 0.1 reduce_max.9
  121.3 10.7 %fusion.4 = f32[4,2,32,32,32,1]{4,3,5,2,1,0:T(8,128)S(1)} fusion(f32[4,2,32,32,2,32,1]{3,5,4,6,2,1,0:T(8,128)} %fusion.6, f32[1,32,32]{2,1,0:T(8,128)S(1)} %get-tuple-element.35, f32[1,32,32]{2,1,0:T(8,128)S(1)} %get-tuple-element.36), kind=kOutput, calls=%fused_computation.5 | convolution fusion | flops 201328640 | bytes 3153920 | tf_op jit(solution)/shard_map/lmq,...qlg->...mg/dot_general | solution.py:82
  132.1 7.1 %fusion.15 = f32[4,2,32,32,2,32]{3,5,4,2,1,0:T(8,128)S(1)} fusion(f32[4,2,32,32,32,1]{4,3,5,2,1,0:T(8,128)S(1)} %fusion.4, f32[4]{0:T(128)S(1)} %get-tuple-element.30, f32[4]{0:T(128)S(1)} %get-tuple-element.29, f32[4]{0:T(128)S(1)} %get-tuple-element.11, f32[32,1,32]{2,0,1:T(8,128)S(1)} %get-tuple-element.33, f32[32,1,32]{2,0,1:T(8,128)S(1)} %get-tuple-element.34), kind=kOutput, calls=%fused_computation.17 | convolution fusion | flops 202639360 | bytes 3153968 | tf_op jit(solution)/shard_map/...uw,wdq->...udq/dot_general | solution.py:54
  139.2 9.3 %fusion.23 = f32[4,2,32,2,32,32]{4,5,3,2,1,0:T(8,128)} fusion(f32[4,2,32,32,2,32]{3,5,4,2,1,0:T(8,128)S(1)} %fusion.15, f32[1,32,2,32]{3,1,2,0:T(8,128)S(1)} %get-tuple-element.28, f32[1,32,2,32]{3,1,2,0:T(8,128)S(1)} %get-tuple-element.27), kind=kOutput, calls=%fused_computation.28 | convolution fusion | flops 402657280 | bytes 4210688 | tf_op jit(solution)/shard_map/cpdu,...udq->...cpq/dot_general | solution.py:61
  148.5 8.9 %copy.78 = f32[4,2,32,2,32,32]{5,4,3,2,1,0:T(8,128)} copy(f32[4,2,32,2,32,32]{4,5,3,2,1,0:T(8,128)} %fusion.23) | data formatting | bytes 4194304 | tf_op jit(solution)/shard_map/cpdu,...udq->...cpq/transpose | solution.py:61
  157.5 7.5 %reshape.502 = f32[4,2,32,2048]{3,2,1,0:T(8,128)} reshape(f32[4,2,32,2,32,32]{5,4,3,2,1,0:T(8,128)} %copy.78) | data formatting | bytes 4194304 | tf_op jit(solution)/shard_map/reshape | solution.py:68
  165.0 1.8 multiply_add_fusion.1
  166.7 0.6 subtract_reduce_fusion.1
  167.3 0.3 multiply_add_fusion.3
  167.6 1.5 pad_maximum_fusion.1
  169.2 6.3 %reshape.537 = f32[4,2,32,2,32,32,1]{5,4,3,2,1,0,6:T(8,128)} reshape(f32[4,2,32,2048]{3,2,1,0:T(8,128)} %pad_maximum_fusion.1) | data formatting | bytes 4194304 | tf_op jit(solution)/shard_map/reshape | solution.py:74
  175.4 22.8 %fusion.2 = f32[4,2,32,32,2,32,1]{3,5,4,6,2,1,0:T(8,128)S(1)} fusion(f32[4,2,32,2,32,32,1]{5,4,3,2,1,0,6:T(8,128)} %reshape.537, f32[1,32,2,32]{3,1,2,0:T(8,128)S(1)} %get-tuple-element.28, f32[1,32,2,32]{3,1,2,0:T(8,128)S(1)} %get-tuple-element.27), kind=kOutput, calls=%fused_computation.3 | convolution fusion | flops 402657280 | bytes 4210688 | tf_op jit(solution)/shard_map/...cpq,cqew->...pew/dot_general | solution.py:75
  198.2 6.6 %fusion = f32[4,2,32,32,32,1]{4,3,5,2,1,0:T(8,128)S(1)} fusion(f32[4,2,32,32,2,32,1]{3,5,4,6,2,1,0:T(8,128)S(1)} %fusion.2, f32[1,32,32]{2,1,0:T(8,128)S(1)} %get-tuple-element.35, f32[1,32,32]{2,1,0:T(8,128)S(1)} %get-tuple-element.36), kind=kOutput, calls=%fused_computation.1 | convolution fusion | flops 201328640 | bytes 3153920 | tf_op jit(solution)/shard_map/lmq,...qlg->...mg/dot_general | solution.py:82
  204.9 8.9 %fusion.13 = f32[4,2,32,32,2,32]{3,5,4,2,1,0:T(8,128)S(1)} fusion(f32[4,2,32,32,32,1]{4,3,5,2,1,0:T(8,128)S(1)} %fusion, f32[4,2,32,32,32,1]{4,3,5,2,1,0:T(8,128)S(1)} %copy-done.1, f32[4]{0:T(128)S(1)} %get-tuple-element.30, f32[4]{0:T(128)S(1)} %get-tuple-element.29, f32[4]{0:T(128)S(1)} %get-tuple-element.11, f32[32,1,32]{2,0,1:T(8,128)S(1)} %get-tuple-element.33, ...), kind=kOutput, calls=%fused_computation.15 | convolution fusion | flops 204474368 | bytes 4202544 | tf_op jit(solution)/shard_map/...uw,wdq->...udq/dot_general | solution.py:54
  213.8 8.9 %fusion.26 = f32[4,2,32,2,32,32]{4,5,3,2,1,0:T(8,128)} fusion(f32[4,2,32,32,2,32]{3,5,4,2,1,0:T(8,128)S(1)} %fusion.13, f32[1,32,2,32]{3,1,2,0:T(8,128)S(1)} %get-tuple-element.28, f32[1,32,2,32]{3,1,2,0:T(8,128)S(1)} %get-tuple-element.27), kind=kOutput, calls=%fused_computation.29 | convolution fusion | flops 402657280 | bytes 4210688 | tf_op jit(solution)/shard_map/cpdu,...udq->...cpq/dot_general | solution.py:61
  222.7 8.9 %copy.83 = f32[4,2,32,2,32,32]{5,4,3,2,1,0:T(8,128)} copy(f32[4,2,32,2,32,32]{4,5,3,2,1,0:T(8,128)} %fusion.26) | data formatting | bytes 4194304 | tf_op jit(solution)/shard_map/cpdu,...udq->...cpq/transpose | solution.py:61
  231.7 7.7 %reshape.504 = f32[4,2,32,2048]{3,2,1,0:T(8,128)} reshape(f32[4,2,32,2,32,32]{5,4,3,2,1,0:T(8,128)} %copy.83) | data formatting | bytes 4194304 | tf_op jit(solution)/shard_map/reshape | solution.py:68
  239.4 2.3 subtract_reduce_fusion
  241.7 0.4 multiply_add_fusion.2
  242.1 0.2 pad_maximum_fusion.2
  242.4 2.7 fusion.72
  245.1 4.4 copy.87
  249.5 4.9 %all-to-all-start.1 = ((f32[8,2,32,2048]{3,2,1,0:T(8,128)}), f32[8,2,32,2048]{3,2,1,0:T(8,128)}, u32[]{:S(2)}, u32[]{:S(2)}) async-start(f32[8,2,32,2048]{3,2,1,0:T(8,128)} %copy.87), calls=%async_computation.1 | async-start | bytes 8388608 | tf_op jit(solution)/shard_map/all_to_all | solution.py:171
  254.5 0.1 reshape.544
  254.6 48.2 %all-to-all-done.1 = f32[8,2,32,2048]{3,2,1,0:T(8,128)} async-done(((f32[8,2,32,2048]{3,2,1,0:T(8,128)}), f32[8,2,32,2048]{3,2,1,0:T(8,128)}, u32[]{:S(2)}, u32[]{:S(2)}) %all-to-all-start.1) | async-done | bytes 4194336 | tf_op jit(solution)/shard_map/all_to_all | solution.py:171
  302.8 3.1 reduce_sum.119
  305.9 0.5 convolution_bitcast_fusion
  306.4 0.3 fusion.39
  306.7 0.7 div.88
  307.4 139.5 %all-reduce.2.cloned.1.call-done = f32[1,32,2048]{2,1,0:T(8,128)} async-done(((f32[1,32,2048]{2,1,0:T(8,128)}), f32[1,32,2048]{2,1,0:T(8,128)}) %all-reduce.2.cloned.1.call-update) | async-done | bytes 262160 | tf_op jit(solution)/shard_map/psum | solution.py:173
  446.9 0.9 dynamic-slice_reduce_fusion
  447.8 0.3 convolution_bitcast_fusion.4
  448.1 0.8 multiply_reduce_fusion
  449.7 0.1 div.96
  449.7 0.6 multiply_reduce_fusion.1
  451.1 0.6 broadcast_divide_fusion
  (35 shorter events, 0.7 us)
Async XLA Ops:
  7.2 21.9 %copy-start.4 = (s32[4,2]{0,1:T(2,128)S(1)}, s32[4,2]{0,1:T(2,128)}, u32[]{:S(2)}) copy-start(s32[4,2]{0,1:T(2,128)} %param.4) | copy-start | bytes 100
  7.2 22.1 %copy-start.3 = (f32[4,1024]{1,0:T(4,128)S(1)}, f32[4,1024]{1,0:T(4,128)}, u32[]{:S(2)}) copy-start(f32[4,1024]{1,0:T(4,128)} %param.3) | copy-start | bytes 49156
  14.4 68.3 %all-to-all-start = ((f32[256,1,1,2048]{3,2,1,0:T(1,128)}), f32[256,1,1,2048]{3,2,1,0:T(1,128)S(1)}, u32[]{:S(2)}, u32[]{:S(2)}) async-start(f32[256,1,1,2048]{3,2,1,0:T(1,128)} %stack.22), calls=%async_computation | async-start | bytes 4194304 | tf_op jit(solution)/shard_map/all_to_all | solution.py:137
  132.0 7.2 %copy-start = (f32[4,2,32,32,32,1]{4,3,5,2,1,0:T(8,128)}, f32[4,2,32,32,32,1]{4,3,5,2,1,0:T(8,128)S(1)}, u32[]{:S(2)}) copy-start(f32[4,2,32,32,32,1]{4,3,5,2,1,0:T(8,128)S(1)} %fusion.4) | copy-start | bytes 3145732
  198.2 6.7 %copy-start.1 = (f32[4,2,32,32,32,1]{4,3,5,2,1,0:T(8,128)S(1)}, f32[4,2,32,32,32,1]{4,3,5,2,1,0:T(8,128)}, u32[]{:S(2)}) copy-start(f32[4,2,32,32,32,1]{4,3,5,2,1,0:T(8,128)} %copy-done) | copy-start | bytes 3145732
  239.4 2.3 copy-start.2
  249.5 53.2 %all-to-all-start.1 = ((f32[8,2,32,2048]{3,2,1,0:T(8,128)}), f32[8,2,32,2048]{3,2,1,0:T(8,128)}, u32[]{:S(2)}, u32[]{:S(2)}) async-start(f32[8,2,32,2048]{3,2,1,0:T(8,128)} %copy.87), calls=%async_computation.1 | async-start | bytes 8388608 | tf_op jit(solution)/shard_map/all_to_all | solution.py:171
  254.4 192.4 %all-reduce.2.cloned.1.call-start = ((), (), s32[]{:S(2)}) async-start(), calls=%async_computation.2 | async-start | bytes 524288 | tf_op jit(solution)/shard_map/psum | solution.py:173
Sparse Core Ops, SparseCore 0:
  306.0 140.8 all-reduce.1
